TPU v7x, 32 devices: a whole 2x2x4 slice. The times are simulated.
32 devices in a mesh: groups: 2 (over y), prompt: 4 (over x, core), resp: 4 (over z).
Axes of the slice: x: 2, y: 2, z: 4, core: 2. Of those that a mesh axis runs over, the one named last changes fastest.
Arguments:
- queries: bfloat16 [8, 4, 32, 8192], P(('groups', 'prompt'), 'resp'), parts along dimension 0, may hold values from -90 to 90
- cotangent: bfloat16 [8, 4, 32, 8192], P(('groups', 'prompt'), 'resp'), parts along dimension 0, may hold values from -6 to 6
- resp_keys: bfloat16 [8, 4, 32, 512], P(('groups', 'prompt'), 'resp'), parts along dimension 0, may hold values from -6 to 6
- resp_values: bfloat16 [8, 4, 32, 512], P(('groups', 'prompt'), 'resp'), parts along dimension 0, may hold values from -6 to 6
- prefix_keys: bfloat16 [8, 512, 512], P(('groups', 'prompt'), 'resp'), parts along dimension 0, may hold values from -5 to 5
- prefix_values: bfloat16 [8, 512, 512], P(('groups', 'prompt'), 'resp'), parts along dimension 0, may hold values from -6 to 6
- counts: int32 [8], P(('groups', 'prompt')), parts along dimension 0, may hold values from 1 to 4, as said below
- lengths: int32 [8, 4], P(('groups', 'prompt'), 'resp'), parts along dimension 0, may hold values from 8 to 32, as said below
- policy_likelihood: float32 [8, 4], P(('groups', 'prompt'), 'resp'), parts along dimension 0, may hold values from -8 to 8
- reference_likelihood: float32 [8, 4], P(('groups', 'prompt'), 'resp'), parts along dimension 0, may hold values from -8 to 8
Outputs:
- grad_queries: bfloat16 [8, 4, 32, 8192], P(('groups', 'prompt'), 'resp'), parts along dimension 0
- grad_resp_keys: bfloat16 [8, 4, 32, 512], P(('groups', 'prompt'), 'resp'), parts along dimension 0
- grad_resp_values: bfloat16 [8, 4, 32, 512], P(('groups', 'prompt'), 'resp'), parts along dimension 0
- grad_prefix_keys: bfloat16 [8, 512, 512], P(('groups', 'prompt'), 'resp'), parts along dimension 0
- grad_prefix_values: bfloat16 [8, 512, 512], P(('groups', 'prompt'), 'resp'), parts along dimension 0
- forget_loss: float32 [8], P(('groups', 'prompt')), parts along dimension 0
There are 2 independent parts, one for each index of `groups`. A program takes and returns all parts, laid end to end along the dimension named above; each array names one. Nothing has to cross between parts.
Inputs may be any that keep to these rules, and one draw needn't show every extreme that they name: `counts`: live responses of a prompt fill its first slots; some prompt has all 4. `lengths`: tokens of a response are its first slots, the rest padding; each prompt has a live response of 32 tokens.
All inputs are finite; a program needn't handle non-finite values.
Results may differ from a plain program's by a relative error of at most 0.0085.
Values may be sent and summed in bfloat16 or wider, within the bound.
No kernel may reach another device: no remote copies, remote signals or barrier semaphores. Data moves between devices by JAX's collectives and lax.ppermute only.
A program may use at most 128 MiB of HBM per device.

v0:
```python
import math
import jax
import jax.numpy as jnp
from jax import lax
from jax.sharding import PartitionSpec as P

HEADS = 64
KV_HEADS = 4
HEAD_DIM = 128
loss_beta = 0.5
masked_score = -1e30


def head_block(values_in, position, column_span):
    return lax.slice_in_dim(
        values_in, position * column_span, (position + 1) * column_span, axis=values_in.ndim - 1
    )


def across_rows(left_side, right_side):
    return lax.dot_general(
        left_side, right_side, (((1,), (1,)), ((), ())), preferred_element_type=jnp.float32
    )


def down_columns(left_side, right_side):
    return lax.dot_general(
        left_side, right_side, (((0,), (0,)), ((), ())), preferred_element_type=jnp.float32
    )


def own_scores(query_four, own_keys, scaling):
    resp_len = own_keys.shape[1]
    scores = (
        jnp.einsum("sqgd,skd->sqgk", query_four, own_keys, preferred_element_type=jnp.float32)
        * scaling
    )
    positions = jnp.arange(resp_len, dtype=jnp.int32)
    causal = positions[:, None] >= positions[None, :]
    return jnp.where(causal[None, :, None, :], scores, masked_score).reshape(-1, resp_len)


def own_slopes(grad_four, own_values):
    resp_len = own_values.shape[1]
    return jnp.einsum(
        "sqgd,skd->sqgk", grad_four, own_values, preferred_element_type=jnp.float32
    ).reshape(-1, resp_len)


def own_grads(shift_own, weights_own, query_four, grad_four, own_keys, scaling):
    four_shape = query_four.shape[:3] + (own_keys.shape[1],)
    shift_four = shift_own.reshape(four_shape)
    weight_four = weights_own.astype(jnp.bfloat16).reshape(four_shape)
    query_grad = (
        jnp.einsum("sqgk,skd->sqgd", shift_four, own_keys, preferred_element_type=jnp.float32)
        * scaling
    )
    key_grad = (
        jnp.einsum("sqgk,sqgd->skd", shift_four, query_four, preferred_element_type=jnp.float32)
        * scaling
    )
    value_grad = jnp.einsum(
        "sqgk,sqgd->skd", weight_four, grad_four, preferred_element_type=jnp.float32
    )
    return (query_grad.reshape(-1, own_keys.shape[2]), key_grad, value_grad)


def on_device(
    queries,
    cotangent,
    resp_keys,
    resp_values,
    prefix_keys,
    prefix_values,
    counts,
    lengths,
    policy_likelihood,
    reference_likelihood,
):
    group_size = HEADS // KV_HEADS
    group_width = group_size * HEAD_DIM
    scaling = 1.0 / math.sqrt(HEAD_DIM)
    slot_count = queries.shape[1]
    resp_len = queries.shape[2]
    local_keys = prefix_keys[0]
    local_values = prefix_values[0]
    prefix_len = local_keys.shape[0] * lax.axis_size("resp")
    live_count = counts[0]
    count_real = live_count.astype(jnp.float32)
    slot_ids = lax.axis_index("resp") * slot_count + jnp.arange(slot_count, dtype=jnp.int32)
    live_slots = slot_ids < live_count
    margin = policy_likelihood[0] - reference_likelihood[0]
    weight = jnp.where(live_slots, 2.0 * jax.nn.sigmoid(loss_beta * margin) / count_real, 0.0)
    loss_terms = jnp.where(live_slots, 2.0 / loss_beta * jax.nn.softplus(loss_beta * margin), 0.0)
    forget_loss = (lax.psum(jnp.sum(loss_terms), "resp") / count_real).reshape(1)
    positions = jnp.arange(resp_len, dtype=jnp.int32)
    kept_tokens = positions[None, :] < lengths[0][:, None]
    factor = jnp.where(kept_tokens, weight[:, None], 0.0)
    grad_out = (cotangent[0].astype(jnp.float32) * factor[:, :, None]).astype(jnp.bfloat16)
    query_fours, grad_fours, query_rows, grad_rows = ([], [], [], [])
    keys_own, scores_own, slopes_own = ([], [], [])
    for group_index in range(KV_HEADS):
        query_four = head_block(queries[0], group_index, group_width).reshape(
            slot_count, resp_len, group_size, HEAD_DIM
        )
        grad_four = head_block(grad_out, group_index, group_width).reshape(
            slot_count, resp_len, group_size, HEAD_DIM
        )
        own_keys = head_block(resp_keys[0], group_index, HEAD_DIM)
        own_values = head_block(resp_values[0], group_index, HEAD_DIM)
        query_fours.append(query_four)
        grad_fours.append(grad_four)
        query_rows.append(query_four.reshape(-1, HEAD_DIM))
        grad_rows.append(grad_four.reshape(-1, HEAD_DIM))
        keys_own.append(own_keys)
        scores_own.append(own_scores(query_four, own_keys, scaling))
        slopes_own.append(own_slopes(grad_four, own_values))
    query_grads, key_grads, value_grads = ([], [], [])
    start_peaks = jnp.stack(
        [jnp.max(scores_own[group_index], axis=1) for group_index in range(KV_HEADS)]
    )
    start_totals = jnp.stack(
        [
            jnp.sum(jnp.exp(scores_own[group_index] - start_peaks[group_index][:, None]), axis=1)
            for group_index in range(KV_HEADS)
        ]
    )
    arrived = lax.all_gather(local_keys, "resp", axis=0, tiled=True)
    peaks_out = []
    totals_out = []
    for add_group_index in range(KV_HEADS):
        scores_pre = (
            across_rows(query_rows[add_group_index], head_block(arrived, add_group_index, HEAD_DIM))
            * scaling
        )
        peaks_new = jnp.maximum(start_peaks[add_group_index], jnp.max(scores_pre, axis=1))
        totals_new = start_totals[add_group_index] * jnp.exp(
            start_peaks[add_group_index] - peaks_new
        ) + jnp.sum(jnp.exp(scores_pre - peaks_new[:, None]), axis=1)
        peaks_out.append(peaks_new)
        totals_out.append(totals_new)
    row_peaks = jnp.stack(peaks_out)
    totals = jnp.stack(totals_out)
    log_total = row_peaks + jnp.log(totals)
    weights_own = [
        jnp.exp(scores_own[group_index] - log_total[group_index][:, None])
        for group_index in range(KV_HEADS)
    ]
    start_centre = jnp.stack(
        [
            jnp.sum(weights_own[group_index] * slopes_own[group_index], axis=1)
            for group_index in range(KV_HEADS)
        ]
    )

    def add_centre(running, arrived):
        piece_keys, piece_values = arrived
        new_centre = []
        for group_index in range(KV_HEADS):
            scores_pre = (
                across_rows(query_rows[group_index], head_block(piece_keys, group_index, HEAD_DIM))
                * scaling
            )
            weights_pre = jnp.exp(scores_pre - log_total[group_index][:, None])
            slope_pre = across_rows(
                grad_rows[group_index], head_block(piece_values, group_index, HEAD_DIM)
            )
            new_centre.append(running[group_index] + jnp.sum(weights_pre * slope_pre, axis=1))
        return jnp.stack(new_centre)

    centre = add_centre(
        start_centre,
        (
            lax.all_gather(local_keys, "resp", axis=0, tiled=True),
            lax.all_gather(local_values, "resp", axis=0, tiled=True),
        ),
    )
    start_query = []
    for group_index in range(KV_HEADS):
        shift_mine = (
            weights_own[group_index] * (slopes_own[group_index] - centre[group_index][:, None])
        ).astype(jnp.bfloat16)
        query_grad, key_grad, value_grad = own_grads(
            shift_mine,
            weights_own[group_index],
            query_fours[group_index],
            grad_fours[group_index],
            keys_own[group_index],
            scaling,
        )
        start_query.append(query_grad)
        key_grads.append(key_grad)
        value_grads.append(value_grad)
    empty_rows = jnp.zeros((prefix_len, KV_HEADS * HEAD_DIM), jnp.float32)

    def add_terms(running, arrived):
        query_in, keys_in, values_in = running
        piece_keys, piece_values = arrived
        query_out, key_cols, value_cols = ([], [], [])
        for group_index in range(KV_HEADS):
            head_keys = head_block(piece_keys, group_index, HEAD_DIM)
            scores_pre = across_rows(query_rows[group_index], head_keys) * scaling
            weights_pre = jnp.exp(scores_pre - log_total[group_index][:, None])
            slope_pre = across_rows(
                grad_rows[group_index], head_block(piece_values, group_index, HEAD_DIM)
            )
            shift_pre = (weights_pre * (slope_pre - centre[group_index][:, None])).astype(
                jnp.bfloat16
            )
            query_out.append(
                query_in[group_index]
                + jnp.dot(shift_pre, head_keys, preferred_element_type=jnp.float32) * scaling
            )
            key_cols.append(down_columns(shift_pre, query_rows[group_index]) * scaling)
            value_cols.append(
                down_columns(weights_pre.astype(jnp.bfloat16), grad_rows[group_index])
            )
        keys_out = jnp.concatenate(key_cols, axis=1)
        values_out = jnp.concatenate(value_cols, axis=1)
        return (jnp.stack(query_out), keys_out, values_out)

    query_sum, partial_keys, partial_values = add_terms(
        (jnp.stack(start_query), empty_rows, empty_rows),
        (
            lax.all_gather(local_keys, "resp", axis=0, tiled=True),
            lax.all_gather(local_values, "resp", axis=0, tiled=True),
        ),
    )
    query_grads = [query_sum[group_index] for group_index in range(KV_HEADS)]
    grad_queries = jnp.concatenate(
        [
            query_grads[group_index].reshape(slot_count, resp_len, group_width)
            for group_index in range(KV_HEADS)
        ],
        axis=2,
    ).astype(jnp.bfloat16)
    grad_resp_keys = jnp.concatenate(key_grads, axis=2).astype(jnp.bfloat16)
    grad_resp_values = jnp.concatenate(value_grads, axis=2).astype(jnp.bfloat16)
    summed_keys, summed_values = (
        lax.psum_scatter(
            partial_keys.astype(jnp.bfloat16), "resp", scatter_dimension=0, tiled=True
        ).astype(jnp.float32),
        lax.psum_scatter(
            partial_values.astype(jnp.bfloat16), "resp", scatter_dimension=0, tiled=True
        ).astype(jnp.float32),
    )
    return (
        grad_queries[None],
        grad_resp_keys[None],
        grad_resp_values[None],
        summed_keys.astype(jnp.bfloat16)[None],
        summed_values.astype(jnp.bfloat16)[None],
        forget_loss,
    )


def solution(mesh):
    placed = (
        P(("groups", "prompt"), "resp", None, None),
        P(("groups", "prompt"), "resp", None, None),
        P(("groups", "prompt"), "resp", None, None),
        P(("groups", "prompt"), "resp", None, None),
        P(("groups", "prompt"), "resp", None),
        P(("groups", "prompt"), "resp", None),
        P(("groups", "prompt")),
        P(("groups", "prompt"), "resp"),
        P(("groups", "prompt"), "resp"),
        P(("groups", "prompt"), "resp"),
    )
    return jax.shard_map(
        on_device,
        mesh=mesh,
        in_specs=placed,
        out_specs=(
            P(("groups", "prompt"), "resp", None, None),
            P(("groups", "prompt"), "resp", None, None),
            P(("groups", "prompt"), "resp", None, None),
            P(("groups", "prompt"), "resp", None),
            P(("groups", "prompt"), "resp", None),
            P(("groups", "prompt")),
        ),
        check_vma=False,
    )
```

profile of v0, /device:TPU:0, one launch (start us, length us, event | category | flops | bytes accessed | tf_op | source)
XLA Modules:
  0.0 151.5 jit_solution(3817466985412128707)
XLA Ops:
  7.2 1.3 slice_bitcast_fusion.27
  8.5 0.7 copy-done.59
  11.8 0.7 reduce_max.113
  17.3 17.4 %all-gather = bf16[1,512,512]{2,1,0:T(8,128)(2,1)S(1)} all-gather(bf16[1,128,512]{2,1,0:T(8,128)(2,1)S(1)} %copy-done.58), channel_id=2, replica_groups=mesh['groups'=2,'prompt'=4,'resp'=4] {'resp'}, dimensions={1}, use_global_device_ids=true | all-gather | bytes 655360 | tf_op jit(solution)/shard_map/all_gather | solution.py:128
  34.9 0.9 slice_bitcast_fusion.23
  35.8 0.7 dot_general.163
  36.6 0.7 dot_general.158
  37.3 0.7 dot_general.153
  38.1 0.7 reshape_reshape.19
  38.8 0.7 reshape_reshape.18
  44.1 0.7 copy-done.25
  45.7 1.2 fusion.74
  52.4 0.9 pad_maximum_fusion.2
  53.2 2.1 %copy.87 = bf16[512,512]{1,0:T(8,128)(2,1)} copy(bf16[512,512]{0,1:T(8,128)(2,1)} %pad_maximum_fusion.2) | data formatting | bytes 1048576
  55.4 19.7 %all-gather.1 = bf16[1,512,512]{2,1,0:T(8,128)(2,1)S(1)} all-gather(bf16[1,128,512]{2,1,0:T(8,128)(2,1)} %param.15), channel_id=3, replica_groups=mesh['groups'=2,'prompt'=4,'resp'=4] {'resp'}, dimensions={1}, use_global_device_ids=true | all-gather | bytes 655360 | tf_op jit(solution)/shard_map/all_gather | solution.py:175
  75.1 3.1 %multiply_reduce_fusion.3 = (f32[512]{0:T(512)}, f32[512,512]{0,1:T(8,128)}) fusion(f32[512,512]{0,1:T(8,128)} %copy-done, f32[512]{0:T(512)S(1)} %bitcast.309, bf16[512,128]{1,0:T(8,128)(2,1)S(1)} %dot_general.148, bf16[512,512]{1,0:T(8,128)(2,1)S(1)} %bitcast.255), kind=kOutput, calls=%fused_computation.80 | convolution fusion | flops 67894784 | bytes 2363392 | tf_op jit(solution)/shard_map/dot_general | solution.py:21
  78.3 1.9 %multiply_reduce_fusion.2 = (f32[512]{0:T(512)}, f32[512,512]{0,1:T(8,128)}) fusion(f32[512,512]{0,1:T(8,128)S(1)} %get-tuple-element.67, f32[512]{0:T(512)S(1)} %bitcast.304, bf16[512,128]{1,0:T(8,128)(2,1)S(1)} %copy-done.18, bf16[512,512]{1,0:T(8,128)(2,1)S(1)} %bitcast.256), kind=kOutput, calls=%fused_computation.77 | convolution fusion | flops 67894784 | bytes 2363392 | tf_op jit(solution)/shard_map/dot_general | solution.py:21
  80.2 1.9 %multiply_reduce_fusion.1 = (f32[512]{0:T(512)}, f32[512,512]{0,1:T(8,128)}) fusion(f32[512,512]{0,1:T(8,128)S(1)} %get-tuple-element.63, f32[512]{0:T(512)S(1)} %bitcast.299, bf16[512,128]{1,0:T(8,128)(2,1)S(1)} %copy-done.20, bf16[512,512]{1,0:T(8,128)(2,1)S(1)} %bitcast.257), kind=kOutput, calls=%fused_computation.74 | convolution fusion | flops 67894784 | bytes 2363392 | tf_op jit(solution)/shard_map/dot_general | solution.py:21
  82.0 1.9 %multiply_reduce_fusion = (f32[512]{0:T(512)}, f32[512,512]{0,1:T(8,128)}) fusion(f32[512,512]{0,1:T(8,128)S(1)} %get-tuple-element.59, f32[512]{0:T(512)S(1)} %bitcast.294, bf16[512,128]{1,0:T(8,128)(2,1)S(1)} %copy-done.22, bf16[512,512]{1,0:T(8,128)(2,1)S(1)} %bitcast.258), kind=kOutput, calls=%fused_computation.71 | convolution fusion | flops 67894784 | bytes 2363392 | tf_op jit(solution)/shard_map/dot_general | solution.py:21
  83.9 0.7 copy.76
  84.7 1.7 %copy.74 = f32[512,32]{0,1:T(8,128)} copy(f32[512,32]{1,0:T(8,128)} %bitcast.252) | data formatting | bytes 131072 | tf_op jit(solution)/shard_map/reshape | solution.py:40
  86.3 1.7 %copy.72 = f32[512,32]{0,1:T(8,128)} copy(f32[512,32]{1,0:T(8,128)} %bitcast.253) | data formatting | bytes 131072 | tf_op jit(solution)/shard_map/reshape | solution.py:40
  88.0 1.7 %copy.70 = f32[512,32]{0,1:T(8,128)} copy(f32[512,32]{1,0:T(8,128)} %bitcast.254) | data formatting | bytes 131072 | tf_op jit(solution)/shard_map/reshape | solution.py:40
  89.7 1.8 %multiply_reduce_fusion.4 = (f32[512]{0:T(512)S(1)}, f32[512,32]{0,1:T(8,128)}) fusion(f32[512,32]{0,1:T(8,128)} %copy.76, f32[512]{0:T(512)S(1)} %bitcast.295, bf16[512,128]{1,0:T(8,128)(2,1)} %dot_general.163, bf16[1,32,512]{2,1,0:T(8,128)(2,1)} %bitcast.313), kind=kOutput, calls=%fused_computation.126 | convolution fusion | flops 4242944 | bytes 274432 | tf_op jit(solution)/shard_map/sqgd,skd->sqgk/dot_general | solution.py:45
  91.5 1.7 %multiply_reduce_fusion.5 = (f32[512]{0:T(512)S(1)}, f32[512,32]{0,1:T(8,128)}) fusion(f32[512,32]{0,1:T(8,128)} %copy.74, f32[512]{0:T(512)S(1)} %bitcast.300, bf16[512,128]{1,0:T(8,128)(2,1)} %dot_general.158, bf16[1,32,512]{2,1,0:T(8,128)(2,1)} %bitcast.314), kind=kOutput, calls=%fused_computation.129 | convolution fusion | flops 4242944 | bytes 274432 | tf_op jit(solution)/shard_map/sqgd,skd->sqgk/dot_general | solution.py:45
  93.2 1.7 %multiply_reduce_fusion.6 = (f32[512]{0:T(512)S(1)}, f32[512,32]{0,1:T(8,128)}) fusion(f32[512,32]{0,1:T(8,128)} %copy.72, f32[512]{0:T(512)S(1)} %bitcast.305, bf16[512,128]{1,0:T(8,128)(2,1)} %dot_general.153, bf16[1,32,512]{2,1,0:T(8,128)(2,1)} %bitcast.315), kind=kOutput, calls=%fused_computation.132 | convolution fusion | flops 4242944 | bytes 274432 | tf_op jit(solution)/shard_map/sqgd,skd->sqgk/dot_general | solution.py:45
  94.9 1.6 %multiply_reduce_fusion.7 = (f32[512]{0:T(512)S(1)}, f32[512,32]{0,1:T(8,128)}) fusion(f32[512,32]{0,1:T(8,128)} %copy.70, f32[512]{0:T(512)S(1)} %bitcast.310, bf16[512,128]{1,0:T(8,128)(2,1)S(1)} %dot_general.148, bf16[1,32,512]{2,1,0:T(8,128)(2,1)} %bitcast.316), kind=kOutput, calls=%fused_computation.135 | convolution fusion | flops 4242944 | bytes 274432 | tf_op jit(solution)/shard_map/sqgd,skd->sqgk/dot_general | solution.py:45
  97.2 1.6 %multiply_convert_fusion.3 = bf16[512,512]{0,1:T(8,128)(2,1)S(1)} fusion(f32[512,512]{0,1:T(8,128)} %get-tuple-element.87, f32[512,512]{0,1:T(8,128)S(1)} %copy-done.1, f32[512]{0:T(512)S(1)} %add.106, f32[512]{0:T(512)S(1)} %bitcast.311), kind=kLoop, calls=%fused_computation.79 | loop fusion | flops 1048576 | bytes 2625536 | tf_op jit(solution)/shard_map/convert_element_type | solution.py:207
  100.1 0.7 copy-done.65
  103.8 0.9 pad_maximum_fusion.1
  104.7 0.8 copy-done.36
  105.7 0.8 copy-done.44
  106.5 0.8 fusion.35
  108.3 0.8 copy-done.42
  109.1 0.8 fusion.34
  110.9 0.8 copy-done.40
  111.6 0.8 fusion.33
  112.4 0.9 convolution_multiply_fusion.11
  113.5 0.8 copy-done.38
  114.2 0.8 fusion.32
  115.0 0.9 convolution_multiply_fusion.9
  118.7 0.7 sub.360
  119.3 0.7 sub.363
  120.1 1.0 fusion.15
  127.3 12.0 %psum.7 = f32[]{:T(128)} all-reduce(f32[]{:T(128)} %bitcast.64), channel_id=1, replica_groups=mesh['groups'=2,'prompt'=4,'resp'=4] {'resp'}, use_global_device_ids=true, to_apply=%region_26.27 | all-reduce | flops 1 | bytes 8 | tf_op jit(solution)/shard_map/psum | solution.py:95
  140.9 0.8 pad_maximum_fusion
  141.7 1.0 copy.88
  142.8 0.8 copy.82
  (254 shorter events, 32.6 us)
Async XLA Ops:
  7.2 134.6 %reduce-scatter.7.cloned.1.call-start = ((), (), s32[]{:S(2)}) async-start(), calls=%async_computation.3 | async-start | bytes 655360
  8.5 1.0 copy-start.37
  10.4 30.2 %copy-start.11 = (f32[32,16,32]{2,1,0:T(8,128)}, f32[32,16,32]{2,1,0:T(8,128)S(1)}, u32[]{:S(2)}) copy-start(f32[32,16,32]{2,1,0:T(8,128)S(1)} %get-tuple-element.61) | copy-start | bytes 196612
  11.8 29.7 %copy-start.13 = (f32[32,16,32]{2,1,0:T(8,128)}, f32[32,16,32]{2,1,0:T(8,128)S(1)}, u32[]{:S(2)}) copy-start(f32[32,16,32]{2,1,0:T(8,128)S(1)} %get-tuple-element.65) | copy-start | bytes 196612
  12.6 4.7 %copy-start.58 = (bf16[1,128,512]{2,1,0:T(8,128)(2,1)S(1)}, bf16[1,128,512]{2,1,0:T(8,128)(2,1)}, u32[]{:S(2)}) copy-start(bf16[1,128,512]{2,1,0:T(8,128)(2,1)} %param.14) | copy-start | bytes 393220
  12.7 22.1 %copy-start.52 = (bf16[1,1,32,8192]{3,2,1,0:T(8,128)(2,1)S(1)}, bf16[1,1,32,8192]{3,2,1,0:T(8,128)(2,1)}, u32[]{:S(2)}) copy-start(bf16[1,1,32,8192]{3,2,1,0:T(8,128)(2,1)} %param.11) | copy-start | bytes 1572868
  13.3 29.2 %copy-start.15 = (f32[32,16,32]{2,1,0:T(8,128)}, f32[32,16,32]{2,1,0:T(8,128)S(1)}, u32[]{:S(2)}) copy-start(f32[32,16,32]{2,1,0:T(8,128)S(1)} %get-tuple-element.69) | copy-start | bytes 196612
  34.7 9.4 %copy-start.6 = (bf16[1,512,512]{2,1,0:T(8,128)(2,1)}, bf16[1,512,512]{2,1,0:T(8,128)(2,1)S(1)}, u32[]{:S(2)}) copy-start(bf16[1,512,512]{2,1,0:T(8,128)(2,1)S(1)} %all-gather) | copy-start | bytes 1572868
  39.6 4.1 %copy-start.27 = (bf16[512,128]{1,0:T(8,128)(2,1)}, bf16[512,128]{1,0:T(8,128)(2,1)S(1)}, u32[]{:S(2)}) copy-start(bf16[512,128]{1,0:T(8,128)(2,1)S(1)} %reshape_reshape.17) | copy-start | bytes 393220
  39.7 3.7 %copy-start.29 = (bf16[512,128]{1,0:T(8,128)(2,1)}, bf16[512,128]{1,0:T(8,128)(2,1)S(1)}, u32[]{:S(2)}) copy-start(bf16[512,128]{1,0:T(8,128)(2,1)S(1)} %reshape_reshape.16) | copy-start | bytes 393220
  43.7 8.3 %copy-start = (f32[512,512]{0,1:T(8,128)}, f32[512,512]{0,1:T(8,128)S(1)}, u32[]{:S(2)}) copy-start(f32[512,512]{0,1:T(8,128)S(1)} %get-tuple-element.71) | copy-start | bytes 3145732
  43.7 1.0 copy-start.25
  45.7 1.2 copy-start.75
  48.7 1.2 copy-start.21
  55.4 88.2 %reduce-scatter.5.cloned.1.call-start = ((), (), s32[]{:S(2)}) async-start(), calls=%async_computation.2 | async-start | bytes 655360 | tf_op jit(solution)/shard_map/reduce_scatter | solution.py:240
  75.1 3.1 %copy-start.18 = (bf16[512,128]{1,0:T(8,128)(2,1)S(1)}, bf16[512,128]{1,0:T(8,128)(2,1)}, u32[]{:S(2)}) copy-start(bf16[512,128]{1,0:T(8,128)(2,1)} %dot_general.153) | copy-start | bytes 393220
  78.3 1.9 %copy-start.20 = (bf16[512,128]{1,0:T(8,128)(2,1)S(1)}, bf16[512,128]{1,0:T(8,128)(2,1)}, u32[]{:S(2)}) copy-start(bf16[512,128]{1,0:T(8,128)(2,1)} %dot_general.158) | copy-start | bytes 393220
  80.2 1.9 %copy-start.22 = (bf16[512,128]{1,0:T(8,128)(2,1)S(1)}, bf16[512,128]{1,0:T(8,128)(2,1)}, u32[]{:S(2)}) copy-start(bf16[512,128]{1,0:T(8,128)(2,1)} %dot_general.163) | copy-start | bytes 393220
  89.7 7.5 %copy-start.1 = (f32[512,512]{0,1:T(8,128)S(1)}, f32[512,512]{0,1:T(8,128)}, u32[]{:S(2)}) copy-start(f32[512,512]{0,1:T(8,128)} %copy-done) | copy-start | bytes 3145732
  97.2 1.6 %copy-start.30 = (bf16[512,128]{1,0:T(8,128)(2,1)S(1)}, bf16[512,128]{1,0:T(8,128)(2,1)}, u32[]{:S(2)}) copy-start(bf16[512,128]{1,0:T(8,128)(2,1)} %copy-done.29) | copy-start | bytes 393220
  97.2 2.6 %copy-start.10 = (f32[512,512]{0,1:T(8,128)S(1)}, f32[512,512]{0,1:T(8,128)}, u32[]{:S(2)}) copy-start(f32[512,512]{0,1:T(8,128)} %get-tuple-element.83) | copy-start | bytes 3145732
  98.8 1.3 copy-start.2
  99.8 1.3 copy-start.9
  100.1 1.7 %copy-start.4 = (bf16[512,512]{0,1:T(8,128)(2,1)}, bf16[512,512]{0,1:T(8,128)(2,1)S(1)}, u32[]{:S(2)}) copy-start(bf16[512,512]{0,1:T(8,128)(2,1)S(1)} %multiply_convert_fusion.2) | copy-start | bytes 1572868
  101.1 1.2 copy-start.26
  101.4 1.3 copy-start.8
  114.2 1.7 %copy-start.48 = (bf16[4,8,16,128]{3,1,2,0:T(8,128)(2,1)S(1)}, bf16[4,8,16,128]{3,1,2,0:T(8,128)(2,1)}, u32[]{:S(2)}) copy-start(bf16[4,8,16,128]{3,1,2,0:T(8,128)(2,1)} %get-tuple-element.36) | copy-start | bytes 393220
  115.0 1.6 %copy-start.47 = (bf16[4,8,16,128]{3,1,2,0:T(8,128)(2,1)S(1)}, bf16[4,8,16,128]{3,1,2,0:T(8,128)(2,1)}, u32[]{:S(2)}) copy-start(bf16[4,8,16,128]{3,1,2,0:T(8,128)(2,1)} %get-tuple-element.37) | copy-start | bytes 393220
  115.0 2.2 %copy-start.46 = (bf16[4,8,16,128]{3,1,2,0:T(8,128)(2,1)S(1)}, bf16[4,8,16,128]{3,1,2,0:T(8,128)(2,1)}, u32[]{:S(2)}) copy-start(bf16[4,8,16,128]{3,1,2,0:T(8,128)(2,1)} %get-tuple-element.38) | copy-start | bytes 393220
  115.0 2.9 %copy-start.45 = (bf16[4,8,16,128]{3,1,2,0:T(8,128)(2,1)S(1)}, bf16[4,8,16,128]{3,1,2,0:T(8,128)(2,1)}, u32[]{:S(2)}) copy-start(bf16[4,8,16,128]{3,1,2,0:T(8,128)(2,1)} %get-tuple-element.39) | copy-start | bytes 393220
  115.9 2.1 %copy-start.71 = (f32[512]{0:T(512)S(1)}, f32[512]{0:T(512)}, u32[]{:S(2)}) copy-start(f32[512]{0:T(512)} %get-tuple-element.24) | copy-start | bytes 6148
  115.9 4.2 %copy-start.3 = (bf16[512,512]{0,1:T(8,128)(2,1)S(1)}, bf16[512,512]{0,1:T(8,128)(2,1)}, u32[]{:S(2)}) copy-start(bf16[512,512]{0,1:T(8,128)(2,1)} %copy-done.2) | copy-start | bytes 1572868
  115.9 4.2 %copy-start.7 = (bf16[1,512,512]{2,1,0:T(8,128)(2,1)S(1)}, bf16[1,512,512]{2,1,0:T(8,128)(2,1)}, u32[]{:S(2)}) copy-start(bf16[1,512,512]{2,1,0:T(8,128)(2,1)} %copy-done.6) | copy-start | bytes 1572868
  117.2 1.4 copy-start.70
  117.2 2.1 %copy-start.69 = (f32[512]{0:T(512)S(1)}, f32[512]{0:T(512)}, u32[]{:S(2)}) copy-start(f32[512]{0:T(512)} %get-tuple-element.26) | copy-start | bytes 6148
  117.2 2.8 %copy-start.68 = (f32[512]{0:T(512)S(1)}, f32[512]{0:T(512)}, u32[]{:S(2)}) copy-start(f32[512]{0:T(512)} %get-tuple-element.27) | copy-start | bytes 6148
  120.1 1.1 copy-start.5
  121.2 0.9 copy-start.31
  122.1 0.9 copy-start.32
  123.1 0.9 copy-start.16
  123.1 1.0 copy-start.51
  123.1 1.0 copy-start.63
  123.4 1.0 copy-start.14
  124.1 0.9 copy-start.62
  124.4 1.0 copy-start.12
  125.0 0.9 copy-start.49
  125.0 0.9 copy-start.61
  126.2 13.0 %copy-start.53 = (bf16[512,128]{1,0:T(8,128)(2,1)S(1)}, bf16[512,128]{1,0:T(8,128)(2,1)}, u32[]{:S(2)}) copy-start(bf16[512,128]{1,0:T(8,128)(2,1)} %fusion.15) | copy-start | bytes 393220
  (38 other events, 30.1 us)
Sparse Core Ops, SparseCore 0:
  55.5 24.7 reduce-scatter.6
  104.9 21.6 reduce-scatter.4
where the time goes:
time: 153 us; the launch traced here: 152 us
  blocking collectives  49.1 us (32%)
  local copies, waits for them, and re-layouts  44.7 us (29%)
  matrix products  29.8 us (19%)
  between operations  19.5 us (13%)
  other arithmetic  8.31 us (5%)
    unnamed x181, local copies, waits for them, and re-layouts  25.9 us
    all_gather x1, blocking collectives, on_device(): lax.all_gather(local_values, 'resp', axis=0, tiled=True)  19.7 us
    all_gather x1, blocking collectives, on_device(): arrived = lax.all_gather(local_keys, 'resp', axis=0, tiled=True)  17.4 us
    psum x1, blocking collectives, on_device(): lax.psum(jnp.sum(loss_terms), 'resp') / count_real  12 us
    dot_general x8, matrix products, across_rows(): lax.dot_general(left_side, right_side, (((1,), (1,)), ((), ())), preferre...  10.9 us
    dot_general x4, matrix products, own_slopes(): jnp.einsum('sqgd,skd->sqgk', grad_four, own_values, preferred_element_typ...  6.84 us
    reshape x4, local copies, waits for them, and re-layouts, own_scores(): jnp.where(causal[None, :, None, :], scores, masked_score)  5.78 us
    dot_general x4, matrix products, own_grads(): jnp.einsum('sqgk,sqgd->skd', shift_four, query_four, preferred_element_ty...  3.16 us
  transfers between devices with their start and end apart: 2, of which 0 were waited for; matrix products, arithmetic and copies ran while one was open for 29% of the time, Pallas kernels for 0%

commit v1 on v0

--- a/solution.py
+++ b/solution.py
@@ -9,6 +9,29 @@
 HEAD_DIM = 128
 loss_beta = 0.5
 masked_score = -1e30
+
+
+def treat_figure_here(chip_axis, inp):
+    plain, opened, block_next = (lax.axis_size(chip_axis), lax.axis_index(chip_axis), inp.shape[0])
+    nodes = []
+    for t in range(plain):
+        nodes.append((t, (t + 1) % plain))
+    crops = []
+    for t in range(plain):
+        crops.append((t, (t - 1) % plain))
+    z1 = jnp.zeros((*inp.shape[:0], plain * block_next, *inp.shape[1:]), inp.dtype)
+    z1 = lax.dynamic_update_slice_in_dim(z1, inp, opened * block_next, axis=0)
+    a_now = b_next = inp
+    current_arr = plain // 2
+    for d in range(1, current_arr + 1):
+        a_now = lax.ppermute(a_now, chip_axis, nodes)
+        z1 = lax.dynamic_update_slice_in_dim(z1, a_now, (opened - d) % plain * block_next, axis=0)
+        if d < plain - current_arr:
+            b_next = lax.ppermute(b_next, chip_axis, crops)
+            z1 = lax.dynamic_update_slice_in_dim(
+                z1, b_next, (opened + d) % plain * block_next, axis=0
+            )
+    return z1
 
 
 def head_block(values_in, position, column_span):
@@ -172,7 +195,7 @@
         start_centre,
         (
             lax.all_gather(local_keys, "resp", axis=0, tiled=True),
-            lax.all_gather(local_values, "resp", axis=0, tiled=True),
+            treat_figure_here("resp", local_values),
         ),
     )
     start_query = []

time: 153 us -> 192 us (1.25)
  waiting for transfers between devices: 0.04 us -> 17.4 us
  local copies, waits for them, and re-layouts: 44.7 us -> 58.8 us
  starting transfers between devices: 0.08 us -> 6.11 us
  matrix products: 29.8 us -> 35 us
  blocking collectives: 49.1 us -> 45.9 us
    reduce_scatter x1, waiting for transfers between devices: 0.01 us -> 14.1 us  [on_device(): lax.psum_scatter(partial_keys.astype(jnp.bfloat16), 'resp', scatter_dimen...]
    ppermute x0 -> x3, starting transfers between devices: none -> 6.03 us  [the longest x2 3.94 us: treat_figure_here(): a_now = lax.ppermute(a_now, chip_axis, nodes)]
    convert_element_type x4, local copies, waits for them, and re-layouts: 0.48 us -> 4.67 us  [on_device(): shift_mine = (weights_own[group_index] * (slopes_own[group_index] - centr...]
    dot_general x4, matrix products: 2.03 us -> 5.95 us  [own_grads(): jnp.einsum('sqgk,skd->sqgd', shift_four, own_keys, preferred_element_type...]
    dynamic_update_slice x0 -> x4, local copies, waits for them, and re-layouts: none -> 3.84 us  [the longest x2 2.25 us: treat_figure_here(): lax.dynamic_update_slice_in_dim(z1, a_now, (opened - d) % plain * block_n...]
    unnamed x181 -> x203, local copies, waits for them, and re-layouts: 25.9 us -> 29.5 us
    sub x4, local copies, waits for them, and re-layouts: 2.13 us -> 5.43 us  [on_device(): scores_own[group_index] - log_total[group_index][:, None]]
    ppermute x0 -> x3, waiting for transfers between devices: none -> 3.18 us  [the longest x2 3.18 us: treat_figure_here(): a_now = lax.ppermute(a_now, chip_axis, nodes)]
  transfers between devices with their start and end apart: 2 -> 5, of which waited for: 0 -> 2; matrix products, arithmetic and copies ran while one was open for 29% -> 43% of each run, Pallas kernels for 0% -> 0%
where the time goes in v1:
time: 192 us; the launch traced here: 190 us
  local copies, waits for them, and re-layouts  58.8 us (31%)
  blocking collectives  45.9 us (24%)
  matrix products  35 us (18%)
  between operations  19.5 us (10%)
  waiting for transfers between devices  17.4 us (9%)
  other arithmetic  7.73 us (4%)
  starting transfers between devices  6.11 us (3%)
    unnamed x203, local copies, waits for them, and re-layouts  29.5 us
    all_gather x1, blocking collectives, on_device(): lax.all_gather(local_values, 'resp', axis=0, tiled=True)  19.5 us
    all_gather x1, blocking collectives, on_device(): arrived = lax.all_gather(local_keys, 'resp', axis=0, tiled=True)  15.6 us
    reduce_scatter x1, waiting for transfers between devices, on_device(): lax.psum_scatter(partial_keys.astype(jnp.bfloat16), 'resp', scatter_dimen...  14.1 us
    psum x1, blocking collectives, on_device(): lax.psum(jnp.sum(loss_terms), 'resp') / count_real  10.8 us
    dot_general x12, matrix products, across_rows(): lax.dot_general(left_side, right_side, (((1,), (1,)), ((), ())), preferre...  10.3 us
    dot_general x4, matrix products, own_slopes(): jnp.einsum('sqgd,skd->sqgk', grad_four, own_values, preferred_element_typ...  6.36 us
    dot_general x4, matrix products, own_grads(): jnp.einsum('sqgk,skd->sqgd', shift_four, own_keys, preferred_element_type...  5.95 us
  transfers between devices with their start and end apart: 5, of which 2 were waited for; matrix products, arithmetic and copies ran while one was open for 43% of the time, Pallas kernels for 0%

profile of v1, /device:TPU:0, one launch (start us, length us, event | category | flops | bytes accessed | tf_op | source)
XLA Modules:
  0.0 190.4 jit_solution(6580974347387769982)
XLA Ops:
  7.2 3.1 %collective-permute-start = (bf16[128,512]{1,0:T(8,128)(2,1)}, bf16[128,512]{1,0:T(8,128)(2,1)}, u32[]{:S(2)}, u32[]{:S(2)}) collective-permute-start(bf16[128,512]{1,0:T(8,128)(2,1)} %bitcast.278), channel_id=1, source_target_pairs={{0,1},{1,2},{2,3},{3,0},{4,5},{5,6},{6,7},{7,4},{8,9},{9,10},{10,1... | collective-permute-start | bytes 393224 | tf_op jit(solution)/shard_map/ppermute | solution.py:27
  10.3 2.1 %collective-permute-start.1 = (bf16[128,512]{1,0:T(8,128)(2,1)}, bf16[128,512]{1,0:T(8,128)(2,1)}, u32[]{:S(2)}, u32[]{:S(2)}) collective-permute-start(bf16[128,512]{1,0:T(8,128)(2,1)} %bitcast.279), channel_id=1, source_target_pairs={{0,3},{1,0},{2,1},{3,2},{4,7},{5,4},{6,5},{7,6},{8,11},{9,8},{10,9... | collective-permute-start | bytes 393224 | tf_op jit(solution)/shard_map/ppermute | solution.py:30
  12.4 1.3 slice_bitcast_fusion.27
  22.5 15.6 %all-gather = bf16[1,512,512]{2,1,0:T(8,128)(2,1)S(1)} all-gather(bf16[1,128,512]{2,1,0:T(8,128)(2,1)S(1)} %copy-done.64), channel_id=2, replica_groups=mesh['groups'=2,'prompt'=4,'resp'=4] {'resp'}, dimensions={1}, use_global_device_ids=true | all-gather | bytes 655360 | tf_op jit(solution)/shard_map/all_gather | solution.py:151
  38.3 0.9 slice_bitcast_fusion.23
  47.5 1.4 fusion.86
  56.6 2.0 %copy.103 = bf16[512,512]{1,0:T(8,128)(2,1)} copy(bf16[512,512]{0,1:T(8,128)(2,1)} %pad_maximum_fusion.2) | data formatting | bytes 1048576
  58.7 19.5 %all-gather.1 = bf16[1,512,512]{2,1,0:T(8,128)(2,1)} all-gather(bf16[1,128,512]{2,1,0:T(8,128)(2,1)} %param.15), channel_id=3, replica_groups=mesh['groups'=2,'prompt'=4,'resp'=4] {'resp'}, dimensions={1}, use_global_device_ids=true | all-gather | bytes 655360 | tf_op jit(solution)/shard_map/all_gather | solution.py:249
  78.2 1.6 copy.109
  83.2 1.7 copy.84
  84.8 1.7 copy.81
  86.5 1.7 copy.78
  88.2 1.4 sub.365
  89.6 1.4 sub.368
  90.9 1.4 sub.371
  92.3 1.4 sub.374
  93.7 2.3 %multiply_reduce_fusion = (f32[512]{0:T(512)}, f32[512,32]{0,1:T(8,128)}) fusion(f32[512,32]{0,1:T(8,128)} %copy.87, f32[512]{0:T(512)S(1)} %bitcast.302, bf16[512,128]{1,0:T(8,128)(2,1)S(1)} %dot_general.174, bf16[1,32,512]{2,1,0:T(8,128)(2,1)} %bitcast.321), kind=kOutput, calls=%fused_computation.138 | convolution fusion | flops 4242944 | bytes 274432 | tf_op jit(solution)/shard_map/sqgd,skd->sqgk/dot_general | solution.py:68
  95.9 1.4 multiply_reduce_fusion.1
  97.3 1.4 multiply_reduce_fusion.2
  98.7 1.4 multiply_reduce_fusion.3
  100.1 0.9 copy-done.45
  101.0 1.0 copy-done.11
  105.8 10.8 %psum.7 = f32[]{:T(128)} all-reduce(f32[]{:T(128)} %bitcast.65), channel_id=1, replica_groups=mesh['groups'=2,'prompt'=4,'resp'=4] {'resp'}, use_global_device_ids=true, to_apply=%region_26.27 | all-reduce | flops 1 | bytes 8 | tf_op jit(solution)/shard_map/psum | solution.py:118
  117.3 0.9 collective-permute-start.2
  118.2 1.6 constant_dynamic-update-slice_fusion.2
  119.8 1.6 constant_dynamic-update-slice_fusion.1
  121.4 3.2 %collective-permute-done.2 = bf16[128,512]{1,0:T(8,128)(2,1)S(1)} collective-permute-done((bf16[128,512]{1,0:T(8,128)(2,1)}, bf16[128,512]{1,0:T(8,128)(2,1)S(1)}, u32[]{:S(2)}, u32[]{:S(2)}) %collective-permute-start.2) | collective-permute-done | bytes 131104 | tf_op jit(solution)/shard_map/ppermute | solution.py:27
  125.2 1.9 fusion.11
  128.0 0.9 fusion.9
  128.9 0.9 fusion.8
  131.0 1.5 copy.85
  132.6 1.8 fusion.45
  134.4 1.6 convolution_multiply_fusion.15
  137.2 1.5 copy.82
  138.7 1.8 fusion.46
  140.5 1.6 convolution_multiply_fusion.17
  143.4 1.5 copy.79
  144.9 1.8 fusion.47
  146.7 1.8 convolution_multiply_fusion.19
  148.6 2.3 %fusion.5 = bf16[512,512]{0,1:T(8,128)(2,1)} fusion(bf16[512,128]{1,0:T(8,128)(2,1)S(1)} %copy-done.21, f32[512,512]{0,1:T(8,128)} %copy-done, f32[512]{0:T(512)S(1)} %copy-done.72, f32[512]{0:T(512)S(1)} %bitcast.320, bf16[512,512]{1,0:T(8,128)(2,1)S(1)} %bitcast.261), kind=kOutput, calls=%fused_computation.17 | convolution fusion | flops 68157440 | bytes 1839104 | tf_op jit(solution)/shard_map/dot_general | solution.py:44
  150.9 1.1 fusion.6
  153.7 0.9 convolution_multiply_fusion.13
  157.9 0.9 pad_maximum_fusion.1
  159.1 1.0 fusion.24
  162.4 0.9 copy-done.47
  165.7 0.8 pad_maximum_fusion
  166.5 1.0 copy.104
  168.3 14.1 %reduce-scatter.5.cloned.1.call-done = bf16[128,512]{1,0:T(8,128)(2,1)} async-done(((bf16[512,512]{1,0:T(8,128)(2,1)}), bf16[128,512]{1,0:T(8,128)(2,1)}) %reduce-scatter.5.cloned.1.call-update) | async-done | bytes 131088 | tf_op jit(solution)/shard_map/reduce_scatter | solution.py:263
  (287 shorter events, 45.1 us)
Async XLA Ops:
  7.2 159.4 %reduce-scatter.7.cloned.1.call-start = ((), (), s32[]{:S(2)}) async-start(), calls=%async_computation.3 | async-start | bytes 655360
  7.2 110.1 %collective-permute-start = (bf16[128,512]{1,0:T(8,128)(2,1)}, bf16[128,512]{1,0:T(8,128)(2,1)}, u32[]{:S(2)}, u32[]{:S(2)}) collective-permute-start(bf16[128,512]{1,0:T(8,128)(2,1)} %bitcast.278), channel_id=1, source_target_pairs={{0,1},{1,2},{2,3},{3,0},{4,5},{5,6},{6,7},{7,4},{8,9},{9,10},{10,1... | collective-permute-start | bytes 393224 | tf_op jit(solution)/shard_map/ppermute | solution.py:27
  10.3 109.5 %collective-permute-start.1 = (bf16[128,512]{1,0:T(8,128)(2,1)}, bf16[128,512]{1,0:T(8,128)(2,1)}, u32[]{:S(2)}, u32[]{:S(2)}) collective-permute-start(bf16[128,512]{1,0:T(8,128)(2,1)} %bitcast.279), channel_id=1, source_target_pairs={{0,3},{1,0},{2,1},{3,2},{4,7},{5,4},{6,5},{7,6},{8,11},{9,8},{10,9... | collective-permute-start | bytes 393224 | tf_op jit(solution)/shard_map/ppermute | solution.py:30
  15.6 27.7 %copy-start.6 = (f32[32,16,32]{2,1,0:T(8,128)}, f32[32,16,32]{2,1,0:T(8,128)S(1)}, u32[]{:S(2)}) copy-start(f32[32,16,32]{2,1,0:T(8,128)S(1)} %get-tuple-element.61) | copy-start | bytes 196612
  17.0 27.2 %copy-start.8 = (f32[32,16,32]{2,1,0:T(8,128)}, f32[32,16,32]{2,1,0:T(8,128)S(1)}, u32[]{:S(2)}) copy-start(f32[32,16,32]{2,1,0:T(8,128)S(1)} %get-tuple-element.65) | copy-start | bytes 196612
  17.8 4.7 %copy-start.64 = (bf16[1,128,512]{2,1,0:T(8,128)(2,1)S(1)}, bf16[1,128,512]{2,1,0:T(8,128)(2,1)}, u32[]{:S(2)}) copy-start(bf16[1,128,512]{2,1,0:T(8,128)(2,1)} %param.14) | copy-start | bytes 393220
  17.8 20.3 %copy-start.58 = (bf16[1,1,32,8192]{3,2,1,0:T(8,128)(2,1)S(1)}, bf16[1,1,32,8192]{3,2,1,0:T(8,128)(2,1)}, u32[]{:S(2)}) copy-start(bf16[1,1,32,8192]{3,2,1,0:T(8,128)(2,1)} %param.11) | copy-start | bytes 1572868
  18.4 26.6 %copy-start.10 = (f32[32,16,32]{2,1,0:T(8,128)}, f32[32,16,32]{2,1,0:T(8,128)S(1)}, u32[]{:S(2)}) copy-start(f32[32,16,32]{2,1,0:T(8,128)S(1)} %get-tuple-element.69) | copy-start | bytes 196612
  38.1 8.6 %copy-start.4 = (bf16[1,512,512]{2,1,0:T(8,128)(2,1)}, bf16[1,512,512]{2,1,0:T(8,128)(2,1)S(1)}, u32[]{:S(2)}) copy-start(bf16[1,512,512]{2,1,0:T(8,128)(2,1)S(1)} %all-gather) | copy-start | bytes 1572868
  42.2 4.4 %copy-start.27 = (bf16[512,128]{1,0:T(8,128)(2,1)}, bf16[512,128]{1,0:T(8,128)(2,1)S(1)}, u32[]{:S(2)}) copy-start(bf16[512,128]{1,0:T(8,128)(2,1)S(1)} %reshape_reshape.18) | copy-start | bytes 393220
  42.3 4.0 %copy-start.29 = (bf16[512,128]{1,0:T(8,128)(2,1)}, bf16[512,128]{1,0:T(8,128)(2,1)S(1)}, u32[]{:S(2)}) copy-start(bf16[512,128]{1,0:T(8,128)(2,1)S(1)} %reshape_reshape.17) | copy-start | bytes 393220
  42.3 3.6 %copy-start.31 = (bf16[512,128]{1,0:T(8,128)(2,1)}, bf16[512,128]{1,0:T(8,128)(2,1)S(1)}, u32[]{:S(2)}) copy-start(bf16[512,128]{1,0:T(8,128)(2,1)S(1)} %reshape_reshape.16) | copy-start | bytes 393220
  47.5 5.5 %copy-start = (f32[512,512]{0,1:T(8,128)}, f32[512,512]{0,1:T(8,128)S(1)}, u32[]{:S(2)}) copy-start(f32[512,512]{0,1:T(8,128)S(1)} %get-tuple-element.63) | copy-start | bytes 3145732
  47.5 1.4 copy-start.87
  58.7 123.8 %reduce-scatter.5.cloned.1.call-start = ((), (), s32[]{:S(2)}) async-start(), calls=%async_computation.2 | async-start | bytes 655360 | tf_op jit(solution)/shard_map/reduce_scatter | solution.py:263
  78.2 1.6 copy-start.53
  93.6 2.3 %copy-start.19 = (bf16[512,128]{1,0:T(8,128)(2,1)S(1)}, bf16[512,128]{1,0:T(8,128)(2,1)}, u32[]{:S(2)}) copy-start(bf16[512,128]{1,0:T(8,128)(2,1)} %dot_general.168) | copy-start | bytes 393220
  93.6 2.3 %copy-start.41 = (f32[512,32]{0,1:T(8,128)S(1)}, f32[512,32]{0,1:T(8,128)}, u32[]{:S(2)}) copy-start(f32[512,32]{0,1:T(8,128)} %copy.84) | copy-start | bytes 196612
  93.7 2.3 %copy-start.70 = (bf16[1,1,32,512]{3,2,1,0:T(8,128)(2,1)S(1)}, bf16[1,1,32,512]{3,2,1,0:T(8,128)(2,1)}, u32[]{:S(2)}) copy-start(bf16[1,1,32,512]{3,2,1,0:T(8,128)(2,1)} %param.13) | copy-start | bytes 98308
  95.9 1.4 copy-start.16
  95.9 1.4 copy-start.39
  97.3 1.4 copy-start.13
  97.3 1.4 copy-start.37
  101.0 3.2 %copy-start.23 = (bf16[512,512]{1,0:T(8,128)(2,1)}, bf16[512,512]{1,0:T(8,128)(2,1)S(1)}, u32[]{:S(2)}) copy-start(bf16[512,512]{1,0:T(8,128)(2,1)S(1)} %constant_dynamic-update-slice_fusion.3) | copy-start | bytes 1572868
  101.0 1.4 copy-start.9
  117.3 9.8 %copy-start.1 = (f32[512,512]{0,1:T(8,128)S(1)}, f32[512,512]{0,1:T(8,128)}, u32[]{:S(2)}) copy-start(f32[512,512]{0,1:T(8,128)} %copy-done) | copy-start | bytes 3145732
  117.3 7.2 %collective-permute-start.2 = (bf16[128,512]{1,0:T(8,128)(2,1)}, bf16[128,512]{1,0:T(8,128)(2,1)S(1)}, u32[]{:S(2)}, u32[]{:S(2)}) collective-permute-start(bf16[128,512]{1,0:T(8,128)(2,1)} %collective-permute-done), channel_id=1, source_target_pairs={{0,1},{1,2},{2,3},{3,0},{4,5},{5,6},{6,7},{7,4},{8,9},{9,10},{10,1... | collective-permute-start | bytes 393224 | tf_op jit(solution)/shard_map/ppermute | solution.py:27
  125.2 1.9 copy-start.20
  125.2 1.9 copy-start.24
  128.9 1.5 copy-start.42
  128.9 1.5 copy-start.63
  132.6 1.8 copy-start.43
  134.3 1.6 copy-start.79
  134.3 1.6 copy-start.83
  134.4 2.2 %copy-start.40 = (f32[512,32]{0,1:T(8,128)S(1)}, f32[512,32]{0,1:T(8,128)}, u32[]{:S(2)}) copy-start(f32[512,32]{0,1:T(8,128)} %copy.81) | copy-start | bytes 196612
  134.4 2.2 %copy-start.62 = (f32[512,32]{0,1:T(8,128)S(1)}, f32[512,32]{0,1:T(8,128)}, u32[]{:S(2)}) copy-start(f32[512,32]{0,1:T(8,128)} %get-tuple-element.77) | copy-start | bytes 196612
  138.7 1.8 copy-start.44
  140.5 1.6 copy-start.78
  140.5 1.6 copy-start.82
  140.5 2.2 %copy-start.38 = (f32[512,32]{0,1:T(8,128)S(1)}, f32[512,32]{0,1:T(8,128)}, u32[]{:S(2)}) copy-start(f32[512,32]{0,1:T(8,128)} %copy.78) | copy-start | bytes 196612
  140.5 2.2 %copy-start.61 = (f32[512,32]{0,1:T(8,128)S(1)}, f32[512,32]{0,1:T(8,128)}, u32[]{:S(2)}) copy-start(f32[512,32]{0,1:T(8,128)} %get-tuple-element.79) | copy-start | bytes 196612
  144.9 3.7 %copy-start.22 = (bf16[1,512,512]{2,1,0:T(8,128)(2,1)S(1)}, bf16[1,512,512]{2,1,0:T(8,128)(2,1)}, u32[]{:S(2)}) copy-start(bf16[1,512,512]{2,1,0:T(8,128)(2,1)} %all-gather.1) | copy-start | bytes 1572868
  146.7 1.8 copy-start.21
  146.7 1.8 copy-start.72
  148.6 2.3 %copy-start.74 = (f32[512]{0:T(512)S(1)}, f32[512]{0:T(512)}, u32[]{:S(2)}) copy-start(f32[512]{0:T(512)} %copy-done.73) | copy-start | bytes 6148
  150.9 1.1 copy-start.76
  153.7 1.3 copy-start.2
  157.9 1.2 copy-start.5
  (52 other events, 43.7 us)
Sparse Core Ops, SparseCore 0:
  58.8 22.9 reduce-scatter.6
  162.5 19.9 reduce-scatter.4
